TPU v7x, 512 devices: a whole 4x8x8 slice. The times are simulated.
512 devices in a mesh: dp: 8 (over z), cent: 64 (over x, y, core).
Axes of the slice: x: 4, y: 8, z: 8, core: 2. Of those that a mesh axis runs over, the one named last changes fastest.
Arguments:
- points: bfloat16 [24576, 1024], P(('dp', 'cent')), may hold values from -6 to 6
- assign: int32 [24576], P(('dp', 'cent')), may hold values from 0 to 32767, as said below
- centroids: float32 [32768, 1024], P('cent'), may hold values from -6 to 6
- counts: int32 [32768], P('cent'), may hold values from 1 to 4
Outputs:
- new_centroids: float32 [32768, 1024], P('cent')
- best: float32 [24576], P(('dp', 'cent'))
Inputs may be any that keep to these rules, and one draw needn't show every extreme that they name: `assign`: split the points into aligned blocks of 3072 points in order (the points of one dp index). In every block, the clusters k * 512 to (k + 1) * 512 - 1 receive exactly 48 points together, for every k.
All inputs are finite; a program needn't handle non-finite values.
Results may differ from a plain program's by a relative error of at most 0.0003.
Values may be sent and summed in bfloat16 or wider, within the bound.
No kernel may reach another device: no remote copies, remote signals or barrier semaphores. Data moves between devices by JAX's collectives and lax.ppermute only.
A program may use at most 128 MiB of HBM per device.

v0:
```python
import jax
import jax.numpy as jnp
from jax import lax
from jax.sharding import PartitionSpec as P


def renorm(merged):
    return merged * lax.rsqrt(jnp.mean(merged * merged, axis=1, keepdims=True) + 1e-05)


def make_per_device(ncent):

    def per_device(points, assign, centroids, counts):
        kdev = centroids.shape[0]
        pdev, width = points.shape
        first = lax.axis_index("cent") * kdev
        weighted = centroids * counts.astype(jnp.float32)[:, None]
        rows = lax.all_gather(points, "cent", axis=0, tiled=True)
        labels = lax.all_to_all(
            jnp.broadcast_to(assign[None], (ncent, pdev)), "cent", 0, 0, tiled=True
        ).reshape(-1)
        local = labels - first
        mine = (local >= 0) & (local < kdev)
        rank = jnp.cumsum(mine.astype(jnp.int32)) - 1
        pick = mine[None, :] & (rank[None, :] == jnp.arange(pdev, dtype=jnp.int32)[:, None])
        where = jnp.sum(
            jnp.where(pick, jnp.arange(rows.shape[0], dtype=jnp.int32)[None, :], 0), axis=1
        )
        picked = jnp.take(rows, where, axis=0)
        picked_label = jnp.take(local, where, axis=0)
        hi = (picked_label // 16).astype(jnp.bfloat16)
        lo = (picked_label % 16).astype(jnp.bfloat16)
        packed = jnp.concatenate(
            [
                picked.astype(jnp.bfloat16),
                hi[:, None],
                lo[:, None],
                jnp.zeros((pdev, 126), jnp.bfloat16),
            ],
            axis=1,
        )
        gathered = lax.all_gather(packed, "dp", axis=0, tiled=True)
        grows = gathered[:, :width]
        glabel = gathered[:, width].astype(jnp.int32) * 16 + gathered[:, width + 1].astype(
            jnp.int32
        )
        onehot = (glabel[None, :] == jnp.arange(kdev, dtype=jnp.int32)[:, None]).astype(
            jnp.bfloat16
        )
        total = jnp.dot(onehot, grows, preferred_element_type=jnp.float32)
        fresh = renorm(weighted + total)
        rounded = fresh.astype(jnp.bfloat16)
        scores = jnp.dot(rows, rounded.T, preferred_element_type=jnp.float32)
        local_best = jnp.max(scores.reshape(ncent, pdev, kdev), axis=2)
        received = lax.all_to_all(local_best, "cent", 0, 0, tiled=True)
        values = points.astype(jnp.float32)
        scale = width * jnp.sqrt(jnp.mean(values * values, axis=1) + 1e-06)
        return (fresh, jnp.max(received / scale[None, :], axis=0))

    return per_device


def solution(mesh):
    placed = (P(("dp", "cent"), None), P(("dp", "cent")), P("cent", None), P("cent"))
    return jax.shard_map(
        make_per_device(mesh.shape["cent"]),
        mesh=mesh,
        in_specs=placed,
        out_specs=(P("cent", None), P(("dp", "cent"))),
        check_vma=False,
    )
```

profile of v0, /device:TPU:1, one launch (start us, length us, event | category | flops | bytes accessed | tf_op | source)
XLA Modules:
  0.0 165.8 jit_solution(1306409276618937855)
XLA Ops:
  7.2 0.7 all-gather.2.cloned.1.call-update
  7.9 1.3 broadcast_in_dim.32
  9.2 11.6 %all-to-all-start = ((s32[64,1,48]{2,1,0:T(1,128)}), s32[64,1,48]{2,1,0:T(1,128)S(1)}, u32[]{:S(2)}, u32[]{:S(2)}) async-start(s32[64,1,48]{2,1,0:T(1,128)} %broadcast_in_dim.32), calls=%async_computation | async-start | bytes 65536 | tf_op jit(solution)/shard_map/all_to_all | solution.py:19
  20.8 1.0 multiply_reduce_fusion.1
  21.8 0.7 convert_element_type.53
  22.5 7.5 %all-to-all-done = s32[64,1,48]{2,1,0:T(1,128)S(1)} async-done(((s32[64,1,48]{2,1,0:T(1,128)}), s32[64,1,48]{2,1,0:T(1,128)S(1)}, u32[]{:S(2)}, u32[]{:S(2)}) %all-to-all-start) | async-done | bytes 12320 | tf_op jit(solution)/shard_map/all_to_all | solution.py:19
  30.1 0.2 subtract_reduce_fusion
  30.3 0.1 reshape.215
  30.3 0.3 reduce-window.9
  30.6 0.1 slice.25
  30.7 0.1 sub.29
  30.8 0.1 slice_reduce_fusion
  30.9 0.1 add_bitcast_fusion
  31.0 0.2 select_reduce_fusion
  31.3 0.1 copy.19
  31.4 0.1 fusion.8
  31.5 0.8 gather_fusion.1
  32.3 0.1 copy.22
  32.4 70.5 %all-gather.2.cloned.1.call-done = bf16[3072,1024]{1,0:T(8,128)(2,1)} async-done(((bf16[48,1024]{1,0:T(8,128)(2,1)}), bf16[3072,1024]{1,0:T(8,128)(2,1)}) %all-gather.2.cloned.1.call-update) | async-done | bytes 6291472 | tf_op jit(solution)/shard_map/all_gather | solution.py:18
  103.0 4.3 %gather_fusion = bf16[48,1024]{1,0:T(8,128)(2,1)S(1)} fusion(bf16[3072,1024]{1,0:T(8,128)(2,1)} %all-gather.2.cloned.1.call-done, s32[1024]{0:T(1024)S(1)} %pad_clamp_fusion), kind=kCustom, calls=%fused_computation | custom fusion | bytes 196800 | tf_op jit(solution)/shard_map/jit(_take)/gather | solution.py:29
  107.3 0.1 broadcast_select_fusion
  107.4 0.1 concatenate.3
  107.5 23.1 %all_gather.7 = bf16[384,1152]{1,0:T(8,128)(2,1)S(1)} all-gather(bf16[48,1152]{1,0:T(8,128)(2,1)S(1)} %concatenate.3), channel_id=1, replica_groups=mesh['dp'=8,'cent'=64] {'dp'}, dimensions={0}, use_global_device_ids=true | all-gather | bytes 995328 | tf_op jit(solution)/shard_map/all_gather | solution.py:42
  130.5 0.2 add_reduce_fusion
  130.8 0.8 multiply_reduce_fusion
  131.6 0.2 broadcast_multiply_fusion
  131.8 1.7 %copy-done.2 = bf16[3072,1024]{1,0:T(8,128)(2,1)S(1)} copy-done((bf16[3072,1024]{1,0:T(8,128)(2,1)S(1)}, bf16[3072,1024]{1,0:T(8,128)(2,1)}, u32[]{:S(2)}) %copy-start.2) | copy-done | bytes 6291480
  133.6 3.8 %convolution_reduce_fusion = f32[3072]{0:T(1024)S(1)} fusion(bf16[3072,1024]{1,0:T(8,128)(2,1)S(1)} %copy-done.2, f32[512,1024]{1,0:T(8,128)S(1)} %broadcast_multiply_fusion), kind=kOutput, calls=%fused_computation.4 | convolution fusion | flops 3223319552 | bytes 8400896 | tf_op jit(solution)/shard_map/dot_general | solution.py:53
  137.3 0.7 all_to_all.13
  138.0 11.1 %all-to-all-start.1 = ((f32[64,1,48]{2,1,0:T(1,128)}), f32[64,1,48]{2,1,0:T(1,128)S(1)}, u32[]{:S(2)}, u32[]{:S(2)}) async-start(f32[64,1,48]{2,1,0:T(1,128)} %bitcast.3), calls=%async_computation.1 | async-start | bytes 65536 | tf_op jit(solution)/shard_map/all_to_all | solution.py:55
  149.1 9.3 %all-to-all-done.1 = f32[64,1,48]{2,1,0:T(1,128)S(1)} async-done(((f32[64,1,48]{2,1,0:T(1,128)}), f32[64,1,48]{2,1,0:T(1,128)S(1)}, u32[]{:S(2)}, u32[]{:S(2)}) %all-to-all-start.1) | async-done | bytes 12320 | tf_op jit(solution)/shard_map/all_to_all | solution.py:55
  158.4 0.5 divide_reduce_fusion
  (14 shorter events, 0.2 us)
Async XLA Ops:
  7.2 123.6 %copy-start.1 = (f32[512,1024]{1,0:T(8,128)S(1)}, f32[512,1024]{1,0:T(8,128)}, u32[]{:S(2)}) copy-start(f32[512,1024]{1,0:T(8,128)} %param.6) | copy-start | bytes 6291460
  7.2 95.8 %all-gather.2.cloned.1.call-start = ((), (), s32[]{:S(2)}) async-start(), calls=%async_computation.2 | async-start | bytes 6389760 | tf_op jit(solution)/shard_map/all_gather | solution.py:18
  9.2 20.9 %all-to-all-start = ((s32[64,1,48]{2,1,0:T(1,128)}), s32[64,1,48]{2,1,0:T(1,128)S(1)}, u32[]{:S(2)}, u32[]{:S(2)}) async-start(s32[64,1,48]{2,1,0:T(1,128)} %broadcast_in_dim.32), calls=%async_computation | async-start | bytes 65536 | tf_op jit(solution)/shard_map/all_to_all | solution.py:19
  130.8 2.8 %copy-start.2 = (bf16[3072,1024]{1,0:T(8,128)(2,1)S(1)}, bf16[3072,1024]{1,0:T(8,128)(2,1)}, u32[]{:S(2)}) copy-start(bf16[3072,1024]{1,0:T(8,128)(2,1)} %all-gather.2.cloned.1.call-done) | copy-start | bytes 18874372
  133.6 3.8 %copy-start = (f32[512,1024]{1,0:T(8,128)}, f32[512,1024]{1,0:T(8,128)S(1)}, u32[]{:S(2)}) copy-start(f32[512,1024]{1,0:T(8,128)S(1)} %broadcast_multiply_fusion) | copy-start | bytes 6291460
  138.0 20.4 %all-to-all-start.1 = ((f32[64,1,48]{2,1,0:T(1,128)}), f32[64,1,48]{2,1,0:T(1,128)S(1)}, u32[]{:S(2)}, u32[]{:S(2)}) async-start(f32[64,1,48]{2,1,0:T(1,128)} %bitcast.3), calls=%async_computation.1 | async-start | bytes 65536 | tf_op jit(solution)/shard_map/all_to_all | solution.py:55
Sparse Core Ops, SparseCore 0:
  11.3 91.5 all-gather.1
where the time goes:
time: 166 us
  waiting for transfers between devices  88.1 us (53%)
  blocking collectives  23.1 us (14%)
  starting transfers between devices  22.7 us (14%)
  between operations  14.2 us (9%)
  local copies, waits for them, and re-layouts  9.42 us (6%)
  matrix products  4.59 us (3%)
  other arithmetic  3.79 us (2%)
    all_gather x1, waiting for transfers between devices, per_device(): rows = lax.all_gather(points, 'cent', axis=0, tiled=True)  70.5 us
    all_gather x1, blocking collectives, per_device(): gathered = lax.all_gather(packed, 'dp', axis=0, tiled=True)  23.1 us
    all_to_all x1, starting transfers between devices, per_device(): lax.all_to_all(jnp.broadcast_to(assign[None], (ncent, pdev)), 'cent', 0,...  11.6 us
    all_to_all x1, starting transfers between devices, per_device(): received = lax.all_to_all(local_best, 'cent', 0, 0, tiled=True)  11.1 us
    all_to_all x1, waiting for transfers between devices, per_device(): received = lax.all_to_all(local_best, 'cent', 0, 0, tiled=True)  9.3 us
    all_to_all x1, waiting for transfers between devices, per_device(): lax.all_to_all(jnp.broadcast_to(assign[None], (ncent, pdev)), 'cent', 0,...  7.53 us
    gather x1, local copies, waits for them, and re-layouts, per_device(): picked = jnp.take(rows, where, axis=0)  4.32 us
    dot_general x1, matrix products, per_device(): scores = jnp.dot(rows, rounded.T, preferred_element_type=jnp.float32)  3.76 us
  transfers between devices with their start and end apart: 3, of which 3 were waited for; matrix products, arithmetic and copies ran while one was open for 3% of the time, Pallas kernels for 0%

commit v1 on v0

--- a/solution.py
+++ b/solution.py
@@ -2,6 +2,13 @@
 import jax.numpy as jnp
 from jax import lax
 from jax.sharding import PartitionSpec as P
+
+
+def drive_the_desk(raw):
+    k_now = jnp.concatenate(
+        lax.all_to_all(jnp.stack([raw for _ in range(lax.axis_size("dp"))]), "dp", 0, 0), axis=0
+    )
+    return k_now
 
 
 def renorm(merged):
@@ -39,7 +46,7 @@
             ],
             axis=1,
         )
-        gathered = lax.all_gather(packed, "dp", axis=0, tiled=True)
+        gathered = drive_the_desk(packed)
         grows = gathered[:, :width]
         glabel = gathered[:, width].astype(jnp.int32) * 16 + gathered[:, width + 1].astype(
             jnp.int32

time: 166 us -> 174 us (1.048)
  waiting for transfers between devices: 88.1 us -> 115 us
  blocking collectives: 23.1 us -> 0 us
  matrix products: 4.59 us -> 8.07 us
  starting transfers between devices: 22.7 us -> 24.8 us
    all_to_all x0 -> x1, waiting for transfers between devices: none -> 25.5 us  [drive_the_desk(): lax.all_to_all(jnp.stack([raw for _ in range(lax.axis_size('dp'))]), 'dp'...]
    all_gather x1 -> x0, blocking collectives: 23.1 us -> none  [per_device(): gathered = lax.all_gather(packed, 'dp', axis=0, tiled=True)]
    all_to_all x0 -> x1, starting transfers between devices: none -> 7.1 us  [drive_the_desk(): lax.all_to_all(jnp.stack([raw for _ in range(lax.axis_size('dp'))]), 'dp'...]
    all_to_all x1, starting transfers between devices: 11.1 us -> 6.05 us  [per_device(): received = lax.all_to_all(local_best, 'cent', 0, 0, tiled=True)]
    dot_general x1, matrix products: 3.76 us -> 7.24 us  [per_device(): scores = jnp.dot(rows, rounded.T, preferred_element_type=jnp.float32)]
  transfers between devices with their start and end apart: 3 -> 4, of which waited for: 3 -> 4; matrix products, arithmetic and copies ran while one was open for 3% -> 2% of each run, Pallas kernels for 0% -> 0%
where the time goes in v1:
time: 174 us; the launch traced here: 173 us
  waiting for transfers between devices  115 us (66%)
  starting transfers between devices  24.8 us (14%)
  between operations  14.2 us (8%)
  local copies, waits for them, and re-layouts  8.69 us (5%)
  matrix products  8.07 us (5%)
  other arithmetic  2.21 us (1%)
    all_gather x1, waiting for transfers between devices, per_device(): rows = lax.all_gather(points, 'cent', axis=0, tiled=True)  70.5 us
    all_to_all x1, waiting for transfers between devices, drive_the_desk(): lax.all_to_all(jnp.stack([raw for _ in range(lax.axis_size('dp'))]), 'dp'...  25.5 us
    all_to_all x1, starting transfers between devices, per_device(): lax.all_to_all(jnp.broadcast_to(assign[None], (ncent, pdev)), 'cent', 0,...  11.6 us
    all_to_all x1, waiting for transfers between devices, per_device(): received = lax.all_to_all(local_best, 'cent', 0, 0, tiled=True)  9.3 us
    all_to_all x1, waiting for transfers between devices, per_device(): lax.all_to_all(jnp.broadcast_to(assign[None], (ncent, pdev)), 'cent', 0,...  9.24 us
    dot_general x1, matrix products, per_device(): scores = jnp.dot(rows, rounded.T, preferred_element_type=jnp.float32)  7.24 us
    all_to_all x1, starting transfers between devices, drive_the_desk(): lax.all_to_all(jnp.stack([raw for _ in range(lax.axis_size('dp'))]), 'dp'...  7.1 us
    all_to_all x1, starting transfers between devices, per_device(): received = lax.all_to_all(local_best, 'cent', 0, 0, tiled=True)  6.05 us
  transfers between devices with their start and end apart: 4, of which 4 were waited for; matrix products, arithmetic and copies ran while one was open for 2% of the time, Pallas kernels for 0%

profile of v1, /device:TPU:1, one launch (start us, length us, event | category | flops | bytes accessed | tf_op | source)
XLA Modules:
  0.0 173.2 jit_solution(11182857427663340190)
XLA Ops:
  7.2 0.7 all-gather.2.cloned.1.call-update
  7.9 1.3 broadcast_in_dim.32
  9.2 11.6 %all-to-all-start = ((s32[64,1,48]{2,1,0:T(1,128)}), s32[64,1,48]{2,1,0:T(1,128)S(1)}, u32[]{:S(2)}, u32[]{:S(2)}) async-start(s32[64,1,48]{2,1,0:T(1,128)} %broadcast_in_dim.32), calls=%async_computation | async-start | bytes 65536 | tf_op jit(solution)/shard_map/all_to_all | solution.py:26
  20.8 9.2 %all-to-all-done = s32[64,1,48]{2,1,0:T(1,128)S(1)} async-done(((s32[64,1,48]{2,1,0:T(1,128)}), s32[64,1,48]{2,1,0:T(1,128)S(1)}, u32[]{:S(2)}, u32[]{:S(2)}) %all-to-all-start) | async-done | bytes 12320 | tf_op jit(solution)/shard_map/all_to_all | solution.py:26
  30.0 0.2 subtract_reduce_fusion
  30.3 0.1 reshape.221
  30.3 0.3 reduce-window.9
  30.6 0.1 slice.25
  30.7 0.1 sub.29
  30.8 0.1 slice_reduce_fusion
  30.9 0.1 add_bitcast_fusion
  31.0 0.2 select_reduce_fusion
  31.3 0.1 copy.24
  31.4 0.1 fusion.8
  31.5 0.8 gather_fusion.1
  32.3 0.1 copy.27
  32.4 70.5 %all-gather.2.cloned.1.call-done = bf16[3072,1024]{1,0:T(8,128)(2,1)} async-done(((bf16[48,1024]{1,0:T(8,128)(2,1)}), bf16[3072,1024]{1,0:T(8,128)(2,1)}) %all-gather.2.cloned.1.call-update) | async-done | bytes 6291472 | tf_op jit(solution)/shard_map/all_gather | solution.py:25
  102.9 4.3 %gather_fusion = bf16[48,1024]{1,0:T(8,128)(2,1)S(1)} fusion(bf16[3072,1024]{1,0:T(8,128)(2,1)} %all-gather.2.cloned.1.call-done, s32[1024]{0:T(1024)S(1)} %pad_clamp_fusion), kind=kCustom, calls=%fused_computation | custom fusion | bytes 196800 | tf_op jit(solution)/shard_map/jit(_take)/gather | solution.py:36
  107.3 0.1 broadcast_select_fusion
  107.4 0.1 concatenate.3
  107.5 1.0 stack.2
  108.4 7.1 %all-to-all-start.1 = ((bf16[8,48,1152]{2,1,0:T(8,128)(2,1)}), bf16[8,48,1152]{2,1,0:T(8,128)(2,1)S(1)}, u32[]{:S(2)}, u32[]{:S(2)}) async-start(bf16[8,48,1152]{2,1,0:T(8,128)(2,1)} %stack.2), calls=%async_computation.1 | async-start | bytes 1769472 | tf_op jit(solution)/shard_map/all_to_all | solution.py:9
  115.6 0.1 multiply_reduce_fusion.1
  115.7 25.5 %all-to-all-done.1 = bf16[8,48,1152]{2,1,0:T(8,128)(2,1)S(1)} async-done(((bf16[8,48,1152]{2,1,0:T(8,128)(2,1)}), bf16[8,48,1152]{2,1,0:T(8,128)(2,1)S(1)}, u32[]{:S(2)}, u32[]{:S(2)}) %all-to-all-start.1) | async-done | bytes 884768 | tf_op jit(solution)/shard_map/all_to_all | solution.py:9
  141.2 0.2 add_reduce_fusion
  141.5 0.8 multiply_reduce_fusion
  142.3 0.2 broadcast_multiply_fusion
  142.5 7.2 %convolution_reduce_fusion = f32[3072]{0:T(1024)S(1)} fusion(bf16[3072,1024]{1,0:T(8,128)(2,1)} %all-gather.2.cloned.1.call-done, f32[512,1024]{1,0:T(8,128)S(1)} %broadcast_multiply_fusion), kind=kOutput, calls=%fused_computation.4 | convolution fusion | flops 3223319552 | bytes 8400896 | tf_op jit(solution)/shard_map/dot_general | solution.py:60
  149.8 0.7 all_to_all.17
  150.5 6.0 %all-to-all-start.2 = ((f32[64,1,48]{2,1,0:T(1,128)}), f32[64,1,48]{2,1,0:T(1,128)S(1)}, u32[]{:S(2)}, u32[]{:S(2)}) async-start(f32[64,1,48]{2,1,0:T(1,128)} %bitcast.4), calls=%async_computation.2 | async-start | bytes 65536 | tf_op jit(solution)/shard_map/all_to_all | solution.py:62
  156.5 9.3 %all-to-all-done.2 = f32[64,1,48]{2,1,0:T(1,128)S(1)} async-done(((f32[64,1,48]{2,1,0:T(1,128)}), f32[64,1,48]{2,1,0:T(1,128)S(1)}, u32[]{:S(2)}, u32[]{:S(2)}) %all-to-all-start.2) | async-done | bytes 12320 | tf_op jit(solution)/shard_map/all_to_all | solution.py:62
  165.8 0.5 divide_reduce_fusion
  (18 shorter events, 0.2 us)
Async XLA Ops:
  7.2 95.8 %all-gather.2.cloned.1.call-start = ((), (), s32[]{:S(2)}) async-start(), calls=%async_computation.3 | async-start | bytes 6389760 | tf_op jit(solution)/shard_map/all_gather | solution.py:25
  9.2 20.9 %all-to-all-start = ((s32[64,1,48]{2,1,0:T(1,128)}), s32[64,1,48]{2,1,0:T(1,128)S(1)}, u32[]{:S(2)}, u32[]{:S(2)}) async-start(s32[64,1,48]{2,1,0:T(1,128)} %broadcast_in_dim.32), calls=%async_computation | async-start | bytes 65536 | tf_op jit(solution)/shard_map/all_to_all | solution.py:26
  32.4 83.2 %copy-start.3 = (s32[512]{0:T(512)S(1)}, s32[512]{0:T(512)}, u32[]{:S(2)}) copy-start(s32[512]{0:T(512)} %param.7) | copy-start | bytes 6148
  32.4 83.2 %copy-start.2 = (bf16[48,1024]{1,0:T(8,128)(2,1)S(1)}, bf16[48,1024]{1,0:T(8,128)(2,1)}, u32[]{:S(2)}) copy-start(bf16[48,1024]{1,0:T(8,128)(2,1)} %param.4) | copy-start | bytes 294916
  32.4 109.0 %copy-start.1 = (f32[512,1024]{1,0:T(8,128)S(1)}, f32[512,1024]{1,0:T(8,128)}, u32[]{:S(2)}) copy-start(f32[512,1024]{1,0:T(8,128)} %param.6) | copy-start | bytes 6291460
  108.4 32.8 %all-to-all-start.1 = ((bf16[8,48,1152]{2,1,0:T(8,128)(2,1)}), bf16[8,48,1152]{2,1,0:T(8,128)(2,1)S(1)}, u32[]{:S(2)}, u32[]{:S(2)}) async-start(bf16[8,48,1152]{2,1,0:T(8,128)(2,1)} %stack.2), calls=%async_computation.1 | async-start | bytes 1769472 | tf_op jit(solution)/shard_map/all_to_all | solution.py:9
  142.5 7.3 %copy-start = (f32[512,1024]{1,0:T(8,128)}, f32[512,1024]{1,0:T(8,128)S(1)}, u32[]{:S(2)}) copy-start(f32[512,1024]{1,0:T(8,128)S(1)} %broadcast_multiply_fusion) | copy-start | bytes 6291460
  150.5 15.4 %all-to-all-start.2 = ((f32[64,1,48]{2,1,0:T(1,128)}), f32[64,1,48]{2,1,0:T(1,128)S(1)}, u32[]{:S(2)}, u32[]{:S(2)}) async-start(f32[64,1,48]{2,1,0:T(1,128)} %bitcast.4), calls=%async_computation.2 | async-start | bytes 65536 | tf_op jit(solution)/shard_map/all_to_all | solution.py:62
Sparse Core Ops, SparseCore 0:
  11.3 91.5 all-gather.1
